TPU v7x, 32 devices: a whole 2x2x4 slice. The times are simulated.
32 devices in a mesh: slab: 8 (over z, x), orient: 4 (over y, core).
Axes of the slice: x: 2, y: 2, z: 4, core: 2. Of those that a mesh axis runs over, the one named last changes fastest.
Arguments:
- tiles: bfloat16 [192, 1, 128, 128], P('slab'), may hold values from -8 to 8
- assigned_worker: int32 [192], P('slab'), may hold values from -1 to 7, as said below
- wedge_mask: int32 [128, 128], replicated, may hold values 0 or 1
- template_volume: float32 [64, 64, 64], replicated, may hold values from -6 to 6
- rotation_samples: int32 [64, 4096], P('orient', 'slab'), may hold values from 0 to 262143
Outputs:
- scores: bfloat16 [192, 128, 128], P('slab', 'orient')
Inputs may be any that keep to these rules, and one draw needn't show every extreme that they name: `assigned_worker`: the occupied slots of each slab index come first. Slab indices 2m and 2m+1 hold 24 occupied slots together, and some slab index has all 24 occupied. The occupied slots, taken in slot order over all slab indices, are dealt to the workers in turn, so every worker receives exactly 12 tiles and at most 3 from one slab index.
All inputs are finite; a program needn't handle non-finite values.
Results may differ from a plain program's by a relative error of at most 0.0085.
Values may be sent and summed in bfloat16 or wider, within the bound.
No kernel may reach another device: no remote copies, remote signals or barrier semaphores. Data moves between devices by JAX's collectives and lax.ppermute only.
A program may use at most 128 MiB of HBM per device.

v0:
```python
import math
import jax
import jax.numpy as jnp
from jax import lax
from jax.sharding import PartitionSpec as P


def partner(block, axis, bit):
    count = lax.axis_size(axis)
    route = []
    for low in range(count):
        high = low | 1 << bit
        if high != low and high < count:
            route += [(low, high), (high, low)]
    return lax.ppermute(block, axis, route)


def tables(length):
    counter = jnp.arange(length, dtype=jnp.int32)
    angles = (counter[:, None] * counter[None, :] % length).astype(jnp.float32) * (
        2.0 * math.pi / length
    )
    return (jnp.cos(angles).astype(jnp.bfloat16), jnp.sin(angles).astype(jnp.bfloat16))


def band_table(length, box_edge):
    counter = jnp.arange(length, dtype=jnp.int32)
    offsets = (counter[None, :] - counter[:, None]) % length
    return (offsets < box_edge).astype(jnp.float32)


def right_mul(values, table):
    return jnp.einsum("...ab,bc->...ac", values, table, preferred_element_type=jnp.float32)


def left_mul(table, values):
    return jnp.einsum("ka,...ab->...kb", table, values, preferred_element_type=jnp.float32)


def forward_two(values, cosine_table, sine_table):
    first_real = right_mul(values, cosine_table).astype(jnp.bfloat16)
    first_imag = (-right_mul(values, sine_table)).astype(jnp.bfloat16)
    second_real = (left_mul(cosine_table, first_real) + left_mul(sine_table, first_imag)).astype(
        jnp.bfloat16
    )
    second_imag = (left_mul(cosine_table, first_imag) - left_mul(sine_table, first_real)).astype(
        jnp.bfloat16
    )
    return (second_real, second_imag)


def inverse_real(real_part, imag_part, cosine_table, sine_table):
    length = real_part.shape[-1]
    first_real = (right_mul(real_part, cosine_table) - right_mul(imag_part, sine_table)).astype(
        jnp.bfloat16
    )
    first_imag = (right_mul(imag_part, cosine_table) + right_mul(real_part, sine_table)).astype(
        jnp.bfloat16
    )
    return (left_mul(cosine_table, first_real) - left_mul(sine_table, first_imag)) * (
        1.0 / (length * length)
    )


def filtered(values, wedge_weight, cosine_table, sine_table):
    spec_real, spec_imag = forward_two(values, cosine_table, sine_table)
    return inverse_real(
        spec_real * wedge_weight, spec_imag * wedge_weight, cosine_table, sine_table
    ).astype(jnp.bfloat16)


def pick_rows(chosen, source):
    counter = jnp.arange(source.shape[0], dtype=jnp.int32)
    selector = (chosen[:, None] == counter[None, :]).astype(source.dtype)
    flat = source.reshape(source.shape[0], -1)
    picked = jnp.dot(selector, flat, preferred_element_type=jnp.float32).astype(source.dtype)
    return picked.reshape((chosen.shape[0],) + source.shape[1:])


def make_templates(
    template_volume, rotation_samples, box_edge, planes, tile_len, cosine_table, sine_table
):
    count = rotation_samples.shape[0]
    sampled_part = jnp.take(template_volume.reshape(-1), rotation_samples, axis=0).astype(
        jnp.bfloat16
    )
    sampled = lax.all_gather(sampled_part, "slab", axis=1, tiled=True)
    sampled = sampled.reshape(count, planes, box_edge, box_edge)
    padded = jnp.pad(sampled, ((0, 0), (0, 0), (0, tile_len - box_edge), (0, tile_len - box_edge)))
    template_norm = jnp.sqrt(
        jnp.sum(jnp.square(sampled.astype(jnp.float32)), axis=(1, 2, 3)) + 1e-05
    )
    spec_real, spec_imag = forward_two(padded, cosine_table, sine_table)
    return (spec_real, spec_imag, template_norm)


def score_tiles(
    slab_field, templ_real, templ_imag, template_norm, cosine_table, sine_table, band_sum, box_edge
):
    planes = slab_field.shape[1]
    field_real, field_imag = forward_two(slab_field, cosine_table, sine_table)
    left_real = field_real.astype(jnp.float32)[:, None]
    left_imag = field_imag.astype(jnp.float32)[:, None]
    right_real = templ_real.astype(jnp.float32)[None]
    right_imag = templ_imag.astype(jnp.float32)[None]
    prod_real = jnp.sum(left_real * right_real + left_imag * right_imag, axis=2).astype(
        jnp.bfloat16
    )
    prod_imag = jnp.sum(left_imag * right_real - left_real * right_imag, axis=2).astype(
        jnp.bfloat16
    )
    correlation = inverse_real(prod_real, prod_imag, cosine_table, sine_table)
    energy = jnp.sum(jnp.square(slab_field.astype(jnp.float32)), axis=1)
    summed = jnp.einsum(
        "ka,nab,lb->nkl", band_sum, energy, band_sum, precision=lax.Precision.HIGHEST
    )
    local_rms = jnp.sqrt(summed / (box_edge * box_edge * planes) + 1e-05)
    ratio = correlation / (local_rms[:, None] * template_norm[None, :, None, None])
    return jnp.max(ratio, axis=1)


def orient_max(best):
    groups = lax.axis_size("orient")
    parts = lax.all_to_all(best, "orient", split_axis=1, concat_axis=0, tiled=True)
    stacked = parts.reshape(groups, best.shape[0], parts.shape[1], parts.shape[2])
    return jnp.max(stacked, axis=0)


def per_device(tiles, assigned_worker, wedge_mask, template_volume, rotation_samples):
    tile_len = tiles.shape[-1]
    planes = tiles.shape[1]
    home_slots = tiles.shape[0]
    work_slots = home_slots // 2
    box_edge = template_volume.shape[0]
    cosine_table, sine_table = tables(tile_len)
    band_sum = band_table(tile_len, box_edge)
    wedge_weight = wedge_mask.astype(jnp.bfloat16)
    templ_real, templ_imag, template_norm = make_templates(
        template_volume, rotation_samples, box_edge, planes, tile_len, cosine_table, sine_table
    )
    occupied = assigned_worker >= 0
    own_count = jnp.sum(occupied.astype(jnp.int32))
    partner_tiles = partner(tiles[work_slots:], "slab", 0)
    counter = jnp.arange(work_slots, dtype=jnp.int32)
    keep_own = (counter < own_count)[:, None, None, None]
    moved_in = pick_rows(counter - own_count, partner_tiles)
    gathered = jnp.where(keep_own, tiles[:work_slots], moved_in)
    slab_field = filtered(gathered, wedge_weight, cosine_table, sine_table)
    best = score_tiles(
        slab_field,
        templ_real,
        templ_imag,
        template_norm,
        cosine_table,
        sine_table,
        band_sum,
        box_edge,
    )
    best_rows = orient_max(best.astype(jnp.bfloat16))
    outgoing = pick_rows(counter + own_count, best_rows)
    returned = partner(outgoing, "slab", 0)
    result = jnp.concatenate([best_rows, returned], axis=0)
    return jnp.where(occupied[:, None, None], result, jnp.zeros_like(result))


def solution(mesh):
    return jax.shard_map(
        per_device,
        mesh=mesh,
        in_specs=(P("slab", None, None, None), P("slab"), P(), P(), P("orient", "slab")),
        out_specs=P("slab", "orient", None),
        check_vma=False,
    )
```

profile of v0, /device:TPU:0, one launch (start us, length us, event | category | flops | bytes accessed | tf_op | source)
XLA Modules:
  0.0 180.5 jit_solution(15834255213761315557)
XLA Ops:
  0.0 1.8 slice.7
  1.8 2.9 %collective-permute-start = (bf16[12,1,128,128]{3,2,1,0:T(8,128)(2,1)}, bf16[12,1,128,128]{3,2,1,0:T(8,128)(2,1)}, u32[]{:S(2)}, u32[]{:S(2)}) collective-permute-start(bf16[12,1,128,128]{3,2,1,0:T(8,128)(2,1)} %slice.7), channel_id=1, source_target_pairs={{0,4},{4,0},{8,12},{12,8},{16,20},{20,16},{24,28},{28,24},{1,5},{5... | collective-permute-start | bytes 1179656 | tf_op jit(solution)/shard_map/ppermute | solution.py:15
  4.7 1.9 %reshape.192 = bf16[262144]{0:T(1024)(128)(2,1)S(1)} reshape(f32[64,64,64]{2,1,0:T(8,128)} %param.8) | data formatting | bytes 1572864 | tf_op jit(solution)/shard_map/reshape | solution.py:84
  6.6 0.8 fusion.131
  7.4 0.0 copy-start.2
  7.4 50.7 %gather_fusion = bf16[8192]{0:T(1024)(128)(2,1)S(1)} fusion(bf16[262144]{0:T(1024)(128)(2,1)S(1)} %reshape.192, s32[8192]{0:T(1024)S(1)} %broadcast_clamp_fusion), kind=kCustom, calls=%fused_computation | custom fusion | bytes 65536 | tf_op jit(solution)/shard_map/jit(_take)/gather | solution.py:84
  58.1 0.0 copy-done.1
  58.2 30.9 %all_gather.3 = bf16[16,4096]{1,0:T(8,128)(2,1)S(1)} all-gather(bf16[16,512]{1,0:T(8,128)(2,1)S(1)} %select_convert_fusion), channel_id=1, replica_groups=mesh['slab'=8,'orient'=4] {'slab'}, dimensions={1}, use_global_device_ids=true | all-gather | bytes 147456 | tf_op jit(solution)/shard_map/all_gather | solution.py:87
  89.0 0.2 reshape.193
  89.3 0.5 fusion.25
  89.8 0.5 convolution_convert_fusion.2
  90.3 0.5 fusion.103
  90.9 0.5 fusion.107
  91.4 0.5 fusion.40
  92.0 0.0 copy-done.3
  92.0 0.6 convert_reduce_fusion
  92.6 0.6 iota_add_fusion
  93.3 0.5 fusion.43
  93.8 0.7 iota_compare_fusion.4
  94.5 0.3 copy.137
  94.8 0.0 copy-done.2
  94.8 0.1 copy.115
  95.0 0.3 copy.131
  95.3 0.1 multiply_reduce_fusion
  95.5 0.0 collective-permute-done
  95.5 1.0 pad.8
  96.5 0.3 copy.171
  96.9 0.3 convolution_convert_fusion
  97.2 0.1 copy.172
  97.3 1.5 convolution_convert_fusion.4
  98.8 1.5 fusion.29
  100.3 0.5 fusion.120
  100.8 0.5 fusion.116
  101.3 0.5 fusion.54
  101.9 1.4 fusion.118
  103.2 0.5 fusion.56
  103.8 1.4 fusion.113
  105.1 2.9 %fusion.50 = f32[12,128,128]{2,1,0:T(8,128)} fusion(f32[12,128,128]{2,1,0:T(8,128)} %fusion.118, bf16[12,128,128]{1,2,0:T(8,128)(2,1)S(1)} %fusion.56), kind=kOutput, calls=%fused_computation.74 | convolution fusion | flops 101548032 | bytes 1966080 | tf_op jit(solution)/shard_map/ka,...ab->...kb/dot_general | solution.py:37
  108.0 2.2 %fusion.34 = bf16[12,128,128]{2,1,0:T(8,128)(2,1)S(1)} fusion(f32[12,128,128]{2,1,0:T(8,128)} %fusion.50, f32[12,128,128]{2,1,0:T(8,128)} %fusion.113, bf16[12,128,128]{1,2,0:T(8,128)(2,1)S(1)} %fusion.54), kind=kOutput, calls=%fused_computation.56 | convolution fusion | flops 102137856 | bytes 2359296 | tf_op jit(solution)/shard_map/ka,...ab->...kb/dot_general | solution.py:37
  110.2 0.5 fusion.35
  110.7 0.5 convolution_convert_fusion.3
  111.2 1.5 fusion.57
  112.7 0.5 fusion.105
  113.2 1.4 fusion.110
  114.6 1.4 fusion.46
  116.0 1.4 copy.134
  117.4 2.5 %fusion.49 = f32[12,128,128]{1,2,0:T(8,128)} fusion(f32[12,128,128]{2,1,0:T(8,128)} %fusion.110, bf16[12,128,128]{2,1,0:T(8,128)(2,1)S(1)} %fusion.35), kind=kOutput, calls=%fused_computation.73 | convolution fusion | flops 51167232 | bytes 1966080 | tf_op jit(solution)/shard_map/ka,...ab->...kb/dot_general | solution.py:37
  119.9 2.3 %copy.128 = f32[12,128,128]{2,1,0:T(8,128)} copy(f32[12,128,128]{1,2,0:T(8,128)} %fusion.49) | data formatting | bytes 1572864 | tf_op jit(solution)/shard_map/mul | solution.py:106
  122.2 6.9 %fusion.2 = f32[12,16,128,128]{3,2,1,0:T(8,128)} fusion(f32[16,128,128]{2,1,0:T(8,128)S(1)} %copy.137, f32[12,128,128]{2,1,0:T(8,128)S(1)} %copy.134, f32[16,128,128]{2,1,0:T(8,128)S(1)} %copy.131, f32[12,128,128]{2,1,0:T(8,128)} %copy.128), kind=kOutput, calls=%fused_computation.9 | convolution fusion | flops 818135040 | bytes 16252928 | tf_op jit(solution)/shard_map/...ab,bc->...ac/dot_general | solution.py:33
  129.1 0.0 copy-done
  129.1 5.8 %fusion.1 = f32[12,16,128,128]{3,2,1,0:T(8,128)} fusion(f32[16,128,128]{2,1,0:T(8,128)S(1)} %copy.137, f32[12,128,128]{2,1,0:T(8,128)S(1)} %copy.134, f32[16,128,128]{2,1,0:T(8,128)S(1)} %copy.131, f32[12,128,128]{2,1,0:T(8,128)S(1)} %copy-done), kind=kOutput, calls=%fused_computation.8 | convolution fusion | flops 818135040 | bytes 16252928 | tf_op jit(solution)/shard_map/...ab,bc->...ac/dot_general | solution.py:33
  134.9 10.1 %fusion.5 = f32[12,16,128,128]{3,2,1,0:T(8,128)} fusion(f32[12,16,128,128]{3,2,1,0:T(8,128)} %fusion.2, f32[16,128,128]{2,1,0:T(8,128)S(1)} %copy.137, f32[12,128,128]{2,1,0:T(8,128)S(1)} %copy.134, f32[16,128,128]{2,1,0:T(8,128)S(1)} %copy.131, f32[12,128,128]{2,1,0:T(8,128)} %copy.128), kind=kOutput, calls=%fused_computation.12 | convolution fusion | flops 1629978624 | bytes 28835840 | tf_op jit(solution)/shard_map/ka,...ab->...kb/dot_general | solution.py:37
  144.9 2.7 %fusion.27 = f32[12,128,128]{2,1,0:T(8,128)} fusion(f32[12,128,128]{1,2,0:T(8,128)} %fusion.57), kind=kOutput, calls=%fused_computation.40 | convolution fusion | flops 302596096 | bytes 1572864 | tf_op jit(solution)/shard_map/ka,nab,lb->nkl/dot_general | solution.py:114
  147.6 2.3 %copy.141 = f32[12,128,128]{1,2,0:T(8,128)} copy(f32[12,128,128]{2,1,0:T(8,128)} %fusion.27) | data formatting | bytes 1572864 | tf_op jit(solution)/shard_map/sqrt | solution.py:117
  150.0 12.2 %fusion = bf16[12,128,128]{1,2,0:T(8,128)(2,1)S(1)} fusion(f32[12,16,128,128]{3,2,1,0:T(8,128)} %fusion.5, f32[16]{0:T(128)S(1)} %add_sqrt_fusion, f32[12,128,128]{1,2,0:T(8,128)} %copy.141, f32[12,16,128,128]{3,2,1,0:T(8,128)} %fusion.1, f32[16,128,128]{2,1,0:T(8,128)S(1)} %copy.137, f32[12,128,128]{2,1,0:T(8,128)S(1)} %copy.134, ...), kind=kOutput, calls=%fused_computation.7 | convolution fusion | flops 1645510656 | bytes 30015552 | tf_op jit(solution)/shard_map/ka,...ab->...kb/dot_general | solution.py:37
  162.2 0.4 copy.142
  162.6 11.5 %all_to_all.12 = bf16[12,128,128]{2,0,1:T(8,128)(2,1)S(1)} all-to-all(bf16[12,128,128]{2,0,1:T(8,128)(2,1)S(1)} %copy.142), channel_id=1, replica_groups=mesh['slab'=8,'orient'=4] {'orient'}, dimensions={1} | all-to-all | bytes 786432 | tf_op jit(solution)/shard_map/all_to_all | solution.py:124
  174.1 0.1 reduce_max.19
  174.2 0.1 copy.174
  174.3 0.2 convolution_convert_fusion.1
  174.6 0.6 collective-permute-start.1
  175.2 4.4 %collective-permute-done.1 = bf16[12,32,128]{2,0,1:T(8,128)(2,1)S(1)} collective-permute-done((bf16[12,32,128]{2,0,1:T(8,128)(2,1)S(1)}, bf16[12,32,128]{2,0,1:T(8,128)(2,1)S(1)}, u32[]{:S(2)}, u32[]{:S(2)}) %collective-permute-start.1) | collective-permute-done | bytes 98336 | tf_op jit(solution)/shard_map/ppermute | solution.py:15
  179.7 0.1 maximum_select_fusion
  179.8 0.7 copy.145
  (15 shorter events, 0.2 us)
Async XLA Ops:
  0.0 58.1 %copy-start.1 = (s32[16,512]{1,0:T(8,128)S(1)}, s32[16,512]{1,0:T(8,128)}, u32[]{:S(2)}) copy-start(s32[16,512]{1,0:T(8,128)} %param.9) | copy-start | bytes 98308
  1.8 93.7 %collective-permute-start = (bf16[12,1,128,128]{3,2,1,0:T(8,128)(2,1)}, bf16[12,1,128,128]{3,2,1,0:T(8,128)(2,1)}, u32[]{:S(2)}, u32[]{:S(2)}) collective-permute-start(bf16[12,1,128,128]{3,2,1,0:T(8,128)(2,1)} %slice.7), channel_id=1, source_target_pairs={{0,4},{4,0},{8,12},{12,8},{16,20},{20,16},{24,28},{28,24},{1,5},{5... | collective-permute-start | bytes 1179656 | tf_op jit(solution)/shard_map/ppermute | solution.py:15
  7.3 84.6 %copy-start.3 = (s32[24]{0:T(128)S(1)}, s32[24]{0:T(128)}, u32[]{:S(2)}) copy-start(s32[24]{0:T(128)} %param.6) | copy-start | bytes 292
  7.4 87.4 %copy-start.2 = (s32[128,128]{1,0:T(8,128)S(1)}, s32[128,128]{1,0:T(8,128)}, u32[]{:S(2)}) copy-start(s32[128,128]{1,0:T(8,128)} %param.7) | copy-start | bytes 196612
  122.2 6.9 %copy-start = (f32[12,128,128]{2,1,0:T(8,128)S(1)}, f32[12,128,128]{2,1,0:T(8,128)}, u32[]{:S(2)}) copy-start(f32[12,128,128]{2,1,0:T(8,128)} %copy.128) | copy-start | bytes 2359300
  174.6 5.0 %collective-permute-start.1 = (bf16[12,32,128]{2,0,1:T(8,128)(2,1)S(1)}, bf16[12,32,128]{2,0,1:T(8,128)(2,1)S(1)}, u32[]{:S(2)}, u32[]{:S(2)}) collective-permute-start(bf16[12,32,128]{2,0,1:T(8,128)(2,1)S(1)} %copy.144), channel_id=1, source_target_pairs={{0,4},{4,0},{8,12},{12,8},{16,20},{20,16},{24,28},{28,24},{1,5},{5... | collective-permute-start | bytes 294920 | tf_op jit(solution)/shard_map/ppermute | solution.py:15
where the time goes:
time: 181 us; the launch traced here: 180 us
  local copies, waits for them, and re-layouts  64.2 us (35%)
  matrix products  62.5 us (35%)
  blocking collectives  42.3 us (23%)
  waiting for transfers between devices  4.44 us (2%)
  starting transfers between devices  3.53 us (2%)
  other arithmetic  3.09 us (2%)
    gather x2, local copies, waits for them, and re-layouts, make_templates(): jnp.take(template_volume.reshape(-1), rotation_samples, axis=0)  50.7 us
    dot_general x16, matrix products, left_mul(): jnp.einsum('ka,...ab->...kb', table, values, preferred_element_type=jnp.f...  37.3 us
    all_gather x1, blocking collectives, make_templates(): sampled = lax.all_gather(sampled_part, 'slab', axis=1, tiled=True)  30.9 us
    dot_general x10, matrix products, right_mul(): jnp.einsum('...ab,bc->...ac', values, table, preferred_element_type=jnp.f...  20.4 us
    all_to_all x1, blocking collectives, orient_max(): lax.all_to_all(best, 'orient', split_axis=1, concat_axis=0, tiled=True)  11.5 us
    ppermute x2, waiting for transfers between devices, partner(): return lax.ppermute(block, axis, route)  4.44 us
    dot_general x2, matrix products, score_tiles(): jnp.einsum('ka,nab,lb->nkl', band_sum, energy, band_sum, precision=lax.Pr...  4.21 us
  transfers between devices with their start and end apart: 2, of which 1 were waited for; matrix products, arithmetic and copies ran while one was open for 33% of the time, Pallas kernels for 0%

commit v1 on v0

--- a/solution.py
+++ b/solution.py
@@ -84,7 +84,29 @@
     sampled_part = jnp.take(template_volume.reshape(-1), rotation_samples, axis=0).astype(
         jnp.bfloat16
     )
-    sampled = lax.all_gather(sampled_part, "slab", axis=1, tiled=True)
+    v_now = lax.axis_index("slab")
+    response = lax.axis_size("slab")
+    res, r2, back = (response, v_now, sampled_part.shape[1])
+    pool = []
+    for t in range(res):
+        pool.append((t, (t + 1) % res))
+    nodes = []
+    for t in range(res):
+        nodes.append((t, (t - 1) % res))
+    sampled = jnp.zeros(
+        (*sampled_part.shape[:1], res * back, *sampled_part.shape[2:]), sampled_part.dtype
+    )
+    sampled = lax.dynamic_update_slice_in_dim(sampled, sampled_part, r2 * back, axis=1)
+    far_arr = outcome_arr = sampled_part
+    piece_now = res // 2
+    for i0 in range(1, piece_now + 1):
+        far_arr = lax.ppermute(far_arr, "slab", pool)
+        sampled = lax.dynamic_update_slice_in_dim(sampled, far_arr, (r2 - i0) % res * back, axis=1)
+        if i0 < res - piece_now:
+            outcome_arr = lax.ppermute(outcome_arr, "slab", nodes)
+            sampled = lax.dynamic_update_slice_in_dim(
+                sampled, outcome_arr, (r2 + i0) % res * back, axis=1
+            )
     sampled = sampled.reshape(count, planes, box_edge, box_edge)
     padded = jnp.pad(sampled, ((0, 0), (0, 0), (0, tile_len - box_edge), (0, tile_len - box_edge)))
     template_norm = jnp.sqrt(

time: 181 us -> 173 us (0.956)
  blocking collectives: 42.3 us -> 11.4 us
  starting transfers between devices: 3.53 us -> 15.7 us
  waiting for transfers between devices: 4.44 us -> 15.3 us
    all_gather x1 -> x0, blocking collectives: 30.9 us -> none  [make_templates(): sampled = lax.all_gather(sampled_part, 'slab', axis=1, tiled=True)]
    ppermute x0 -> x7, starting transfers between devices: none -> 15.6 us  [the longest x3 8.05 us: make_templates(): outcome_arr = lax.ppermute(outcome_arr, 'slab', nodes)]
    ppermute x0 -> x7, waiting for transfers between devices: none -> 10.4 us  [the longest x4 10.4 us: make_templates(): far_arr = lax.ppermute(far_arr, 'slab', pool)]
    ppermute x2, starting transfers between devices: 3.53 us -> 0.07 us  [partner(): return lax.ppermute(block, axis, route)]
  transfers between devices with their start and end apart: 2 -> 9, of which waited for: 1 -> 4; matrix products, arithmetic and copies ran while one was open for 33% -> 4% of each run, Pallas kernels for 0% -> 0%
where the time goes in v1:
time: 173 us; the launch traced here: 172 us
  local copies, waits for them, and re-layouts  63.4 us (37%)
  matrix products  62.9 us (36%)
  starting transfers between devices  15.7 us (9%)
  waiting for transfers between devices  15.3 us (9%)
  blocking collectives  11.4 us (7%)
  other arithmetic  3.1 us (2%)
    gather x2, local copies, waits for them, and re-layouts, make_templates(): jnp.take(template_volume.reshape(-1), rotation_samples, axis=0)  50.7 us
    dot_general x16, matrix products, left_mul(): jnp.einsum('ka,...ab->...kb', table, values, preferred_element_type=jnp.f...  37.5 us
    dot_general x10, matrix products, right_mul(): jnp.einsum('...ab,bc->...ac', values, table, preferred_element_type=jnp.f...  20.7 us
    all_to_all x1, blocking collectives, orient_max(): lax.all_to_all(best, 'orient', split_axis=1, concat_axis=0, tiled=True)  11.4 us
    ppermute x4, waiting for transfers between devices, make_templates(): far_arr = lax.ppermute(far_arr, 'slab', pool)  10.4 us
    ppermute x3, starting transfers between devices, make_templates(): outcome_arr = lax.ppermute(outcome_arr, 'slab', nodes)  8.05 us
    ppermute x4, starting transfers between devices, make_templates(): far_arr = lax.ppermute(far_arr, 'slab', pool)  7.57 us
    ppermute x2, waiting for transfers between devices, partner(): return lax.ppermute(block, axis, route)  4.94 us
  transfers between devices with their start and end apart: 9, of which 4 were waited for; matrix products, arithmetic and copies ran while one was open for 4% of the time, Pallas kernels for 0%

profile of v1, /device:TPU:0, one launch (start us, length us, event | category | flops | bytes accessed | tf_op | source)
XLA Modules:
  0.0 172.3 jit_solution(15229183943070690743)
XLA Ops:
  0.0 1.9 %reshape.192 = bf16[262144]{0:T(1024)(128)(2,1)S(1)} reshape(f32[64,64,64]{2,1,0:T(8,128)} %param.8) | data formatting | bytes 1572864 | tf_op jit(solution)/shard_map/reshape | solution.py:84
  2.0 0.8 fusion.131
  2.8 50.7 %gather_fusion = bf16[8192]{0:T(1024)(128)(2,1)S(1)} fusion(bf16[262144]{0:T(1024)(128)(2,1)S(1)} %reshape.192, s32[8192]{0:T(1024)S(1)} %broadcast_clamp_fusion), kind=kCustom, calls=%fused_computation | custom fusion | bytes 65536 | tf_op jit(solution)/shard_map/jit(_take)/gather | solution.py:84
  53.6 3.0 %collective-permute-start.1 = (bf16[16,512]{1,0:T(8,128)(2,1)S(1)}, bf16[16,512]{1,0:T(8,128)(2,1)S(1)}, u32[]{:S(2)}, u32[]{:S(2)}) collective-permute-start(bf16[16,512]{1,0:T(8,128)(2,1)S(1)} %get-tuple-element.6), channel_id=1, source_target_pairs={{0,4},{4,8},{8,12},{12,16},{16,20},{20,24},{24,28},{28,0},{1,5},{5... | collective-permute-start | bytes 49160 | tf_op jit(solution)/shard_map/ppermute | solution.py:103
  56.6 3.1 %collective-permute-start.2 = (bf16[16,512]{1,0:T(8,128)(2,1)S(1)}, bf16[16,512]{1,0:T(8,128)(2,1)S(1)}, u32[]{:S(2)}, u32[]{:S(2)}) collective-permute-start(bf16[16,512]{1,0:T(8,128)(2,1)S(1)} %get-tuple-element.6), channel_id=1, source_target_pairs={{0,28},{4,0},{8,4},{12,8},{16,12},{20,16},{24,20},{28,24},{1,29},{... | collective-permute-start | bytes 49160 | tf_op jit(solution)/shard_map/ppermute | solution.py:106
  59.7 0.8 slice.7
  60.5 0.6 convert_reduce_fusion
  61.1 0.6 iota_add_fusion
  61.8 0.7 iota_compare_fusion.4
  62.6 0.1 copy.115
  62.7 2.1 %collective-permute-start.3 = (bf16[16,512]{1,0:T(8,128)(2,1)S(1)}, bf16[16,512]{1,0:T(8,128)(2,1)S(1)}, u32[]{:S(2)}, u32[]{:S(2)}) collective-permute-start(bf16[16,512]{1,0:T(8,128)(2,1)S(1)} %collective-permute-done.1), channel_id=1, source_target_pairs={{0,4},{4,8},{8,12},{12,16},{16,20},{20,24},{24,28},{28,0},{1,5},{5... | collective-permute-start | bytes 49160 | tf_op jit(solution)/shard_map/ppermute | solution.py:103
  64.8 2.7 %collective-permute-start.4 = (bf16[16,512]{1,0:T(8,128)(2,1)S(1)}, bf16[16,512]{1,0:T(8,128)(2,1)S(1)}, u32[]{:S(2)}, u32[]{:S(2)}) collective-permute-start(bf16[16,512]{1,0:T(8,128)(2,1)S(1)} %collective-permute-done.2), channel_id=1, source_target_pairs={{0,28},{4,0},{8,4},{12,8},{16,12},{20,16},{24,20},{28,24},{1,29},{... | collective-permute-start | bytes 49160 | tf_op jit(solution)/shard_map/ppermute | solution.py:106
  67.5 2.2 %collective-permute-done.3 = bf16[16,512]{1,0:T(8,128)(2,1)S(1)} collective-permute-done((bf16[16,512]{1,0:T(8,128)(2,1)S(1)}, bf16[16,512]{1,0:T(8,128)(2,1)S(1)}, u32[]{:S(2)}, u32[]{:S(2)}) %collective-permute-start.3) | collective-permute-done | bytes 16416 | tf_op jit(solution)/shard_map/ppermute | solution.py:103
  69.7 2.5 %collective-permute-start.5 = (bf16[16,512]{1,0:T(8,128)(2,1)S(1)}, bf16[16,512]{1,0:T(8,128)(2,1)S(1)}, u32[]{:S(2)}, u32[]{:S(2)}) collective-permute-start(bf16[16,512]{1,0:T(8,128)(2,1)S(1)} %collective-permute-done.3), channel_id=1, source_target_pairs={{0,4},{4,8},{8,12},{12,16},{16,20},{20,24},{24,28},{28,0},{1,5},{5... | collective-permute-start | bytes 49160 | tf_op jit(solution)/shard_map/ppermute | solution.py:103
  72.2 2.2 %collective-permute-start.6 = (bf16[16,512]{1,0:T(8,128)(2,1)S(1)}, bf16[16,512]{1,0:T(8,128)(2,1)S(1)}, u32[]{:S(2)}, u32[]{:S(2)}) collective-permute-start(bf16[16,512]{1,0:T(8,128)(2,1)S(1)} %collective-permute-done.4), channel_id=1, source_target_pairs={{0,28},{4,0},{8,4},{12,8},{16,12},{20,16},{24,20},{28,24},{1,29},{... | collective-permute-start | bytes 49160 | tf_op jit(solution)/shard_map/ppermute | solution.py:106
  74.5 1.7 collective-permute-done.5
  76.2 6.4 %collective-permute-done.7 = bf16[16,512]{1,0:T(8,128)(2,1)S(1)} collective-permute-done((bf16[16,512]{1,0:T(8,128)(2,1)S(1)}, bf16[16,512]{1,0:T(8,128)(2,1)S(1)}, u32[]{:S(2)}, u32[]{:S(2)}) %collective-permute-start.7) | collective-permute-done | bytes 16416 | tf_op jit(solution)/shard_map/ppermute | solution.py:103
  82.6 0.2 reshape.193
  82.9 0.5 fusion.25
  83.4 0.5 convolution_convert_fusion.2
  83.9 0.5 fusion.103
  84.5 0.5 fusion.107
  85.0 0.5 fusion.40
  85.6 0.5 fusion.43
  86.1 0.3 copy.137
  86.5 0.3 copy.131
  86.8 0.1 multiply_reduce_fusion
  87.0 1.0 pad.8
  88.0 0.3 copy.171
  88.4 0.3 convolution_convert_fusion
  88.7 0.1 copy.172
  88.8 1.5 convolution_convert_fusion.4
  90.3 1.5 fusion.29
  91.8 0.5 fusion.120
  92.3 0.5 fusion.116
  92.8 0.5 fusion.54
  93.3 1.4 fusion.118
  94.7 0.5 fusion.56
  95.2 1.4 fusion.113
  96.7 2.8 %fusion.50 = f32[12,128,128]{2,1,0:T(8,128)} fusion(f32[12,128,128]{2,1,0:T(8,128)} %fusion.118, bf16[12,128,128]{1,2,0:T(8,128)(2,1)S(1)} %fusion.56), kind=kOutput, calls=%fused_computation.74 | convolution fusion | flops 101548032 | bytes 1966080 | tf_op jit(solution)/shard_map/ka,...ab->...kb/dot_general | solution.py:37
  99.5 2.2 %fusion.34 = bf16[12,128,128]{2,1,0:T(8,128)(2,1)S(1)} fusion(f32[12,128,128]{2,1,0:T(8,128)} %fusion.50, f32[12,128,128]{2,1,0:T(8,128)} %fusion.113, bf16[12,128,128]{1,2,0:T(8,128)(2,1)S(1)} %fusion.54), kind=kOutput, calls=%fused_computation.56 | convolution fusion | flops 102137856 | bytes 2359296 | tf_op jit(solution)/shard_map/ka,...ab->...kb/dot_general | solution.py:37
  101.7 0.5 fusion.35
  102.2 0.5 convolution_convert_fusion.3
  102.7 1.5 fusion.57
  104.2 0.5 fusion.105
  104.7 1.4 fusion.110
  106.1 1.4 fusion.46
  107.5 1.4 copy.134
  108.9 2.7 %fusion.49 = f32[12,128,128]{1,2,0:T(8,128)} fusion(f32[12,128,128]{2,1,0:T(8,128)} %fusion.110, bf16[12,128,128]{2,1,0:T(8,128)(2,1)S(1)} %fusion.35), kind=kOutput, calls=%fused_computation.73 | convolution fusion | flops 51167232 | bytes 1966080 | tf_op jit(solution)/shard_map/ka,...ab->...kb/dot_general | solution.py:37
  111.6 2.3 %copy.128 = f32[12,128,128]{2,1,0:T(8,128)} copy(f32[12,128,128]{1,2,0:T(8,128)} %fusion.49) | data formatting | bytes 1572864 | tf_op jit(solution)/shard_map/mul | solution.py:128
  113.9 7.0 %fusion.2 = f32[12,16,128,128]{3,2,1,0:T(8,128)} fusion(f32[16,128,128]{2,1,0:T(8,128)S(1)} %copy.137, f32[12,128,128]{2,1,0:T(8,128)S(1)} %copy.134, f32[16,128,128]{2,1,0:T(8,128)S(1)} %copy.131, f32[12,128,128]{2,1,0:T(8,128)} %copy.128), kind=kOutput, calls=%fused_computation.9 | convolution fusion | flops 818135040 | bytes 16252928 | tf_op jit(solution)/shard_map/...ab,bc->...ac/dot_general | solution.py:33
  120.9 5.8 %fusion.1 = f32[12,16,128,128]{3,2,1,0:T(8,128)} fusion(f32[16,128,128]{2,1,0:T(8,128)S(1)} %copy.137, f32[12,128,128]{2,1,0:T(8,128)S(1)} %copy.134, f32[16,128,128]{2,1,0:T(8,128)S(1)} %copy.131, f32[12,128,128]{2,1,0:T(8,128)S(1)} %copy-done), kind=kOutput, calls=%fused_computation.8 | convolution fusion | flops 818135040 | bytes 16252928 | tf_op jit(solution)/shard_map/...ab,bc->...ac/dot_general | solution.py:33
  126.8 10.1 %fusion.5 = f32[12,16,128,128]{3,2,1,0:T(8,128)} fusion(f32[12,16,128,128]{3,2,1,0:T(8,128)} %fusion.2, f32[16,128,128]{2,1,0:T(8,128)S(1)} %copy.137, f32[12,128,128]{2,1,0:T(8,128)S(1)} %copy.134, f32[16,128,128]{2,1,0:T(8,128)S(1)} %copy.131, f32[12,128,128]{2,1,0:T(8,128)} %copy.128), kind=kOutput, calls=%fused_computation.12 | convolution fusion | flops 1629978624 | bytes 28835840 | tf_op jit(solution)/shard_map/ka,...ab->...kb/dot_general | solution.py:37
  136.8 2.7 %fusion.27 = f32[12,128,128]{2,1,0:T(8,128)} fusion(f32[12,128,128]{1,2,0:T(8,128)} %fusion.57), kind=kOutput, calls=%fused_computation.40 | convolution fusion | flops 302596096 | bytes 1572864 | tf_op jit(solution)/shard_map/ka,nab,lb->nkl/dot_general | solution.py:136
  139.5 2.3 %copy.141 = f32[12,128,128]{1,2,0:T(8,128)} copy(f32[12,128,128]{2,1,0:T(8,128)} %fusion.27) | data formatting | bytes 1572864 | tf_op jit(solution)/shard_map/sqrt | solution.py:139
  141.8 12.2 %fusion = bf16[12,128,128]{1,2,0:T(8,128)(2,1)S(1)} fusion(f32[12,16,128,128]{3,2,1,0:T(8,128)} %fusion.5, f32[16]{0:T(128)S(1)} %add_sqrt_fusion, f32[12,128,128]{1,2,0:T(8,128)} %copy.141, f32[12,16,128,128]{3,2,1,0:T(8,128)} %fusion.1, f32[16,128,128]{2,1,0:T(8,128)S(1)} %copy.137, f32[12,128,128]{2,1,0:T(8,128)S(1)} %copy.134, ...), kind=kOutput, calls=%fused_computation.7 | convolution fusion | flops 1645510656 | bytes 30015552 | tf_op jit(solution)/shard_map/ka,...ab->...kb/dot_general | solution.py:37
  154.0 0.4 copy.142
  154.5 11.4 %all_to_all.12 = bf16[12,128,128]{2,0,1:T(8,128)(2,1)S(1)} all-to-all(bf16[12,128,128]{2,0,1:T(8,128)(2,1)S(1)} %copy.142), channel_id=1, replica_groups=mesh['slab'=8,'orient'=4] {'orient'}, dimensions={1} | all-to-all | bytes 786432 | tf_op jit(solution)/shard_map/all_to_all | solution.py:146
  165.9 0.1 reduce_max.19
  166.1 0.2 convolution_convert_fusion.1
  166.5 0.1 collective-permute-start.8
  166.6 4.9 %collective-permute-done.8 = bf16[12,32,128]{2,0,1:T(8,128)(2,1)S(1)} collective-permute-done((bf16[12,32,128]{2,0,1:T(8,128)(2,1)S(1)}, bf16[12,32,128]{2,0,1:T(8,128)(2,1)S(1)}, u32[]{:S(2)}, u32[]{:S(2)}) %collective-permute-start.8) | collective-permute-done | bytes 98336 | tf_op jit(solution)/shard_map/ppermute | solution.py:15
  171.5 0.1 maximum_select_fusion
  171.6 0.7 copy.145
  (38 shorter events, 0.3 us)
Async XLA Ops:
  0.0 53.5 %copy-start.2 = (s32[16,512]{1,0:T(8,128)S(1)}, s32[16,512]{1,0:T(8,128)}, u32[]{:S(2)}) copy-start(s32[16,512]{1,0:T(8,128)} %param.9) | copy-start | bytes 98308
  0.0 59.7 %copy-start.1 = (bf16[24,1,128,128]{3,2,1,0:T(8,128)(2,1)S(1)}, bf16[24,1,128,128]{3,2,1,0:T(8,128)(2,1)}, u32[]{:S(2)}) copy-start(bf16[24,1,128,128]{3,2,1,0:T(8,128)(2,1)} %param.5) | copy-start | bytes 2359300
  0.0 60.5 %copy-start.4 = (s32[24]{0:T(128)S(1)}, s32[24]{0:T(128)}, u32[]{:S(2)}) copy-start(s32[24]{0:T(128)} %param.6) | copy-start | bytes 292
  0.0 62.5 %copy-start.3 = (s32[128,128]{1,0:T(8,128)S(1)}, s32[128,128]{1,0:T(8,128)}, u32[]{:S(2)}) copy-start(s32[128,128]{1,0:T(8,128)} %param.7) | copy-start | bytes 196612
  53.6 9.1 %collective-permute-start.1 = (bf16[16,512]{1,0:T(8,128)(2,1)S(1)}, bf16[16,512]{1,0:T(8,128)(2,1)S(1)}, u32[]{:S(2)}, u32[]{:S(2)}) collective-permute-start(bf16[16,512]{1,0:T(8,128)(2,1)S(1)} %get-tuple-element.6), channel_id=1, source_target_pairs={{0,4},{4,8},{8,12},{12,16},{16,20},{20,24},{24,28},{28,0},{1,5},{5... | collective-permute-start | bytes 49160 | tf_op jit(solution)/shard_map/ppermute | solution.py:103
  56.6 8.2 %collective-permute-start.2 = (bf16[16,512]{1,0:T(8,128)(2,1)S(1)}, bf16[16,512]{1,0:T(8,128)(2,1)S(1)}, u32[]{:S(2)}, u32[]{:S(2)}) collective-permute-start(bf16[16,512]{1,0:T(8,128)(2,1)S(1)} %get-tuple-element.6), channel_id=1, source_target_pairs={{0,28},{4,0},{8,4},{12,8},{16,12},{20,16},{24,20},{28,24},{1,29},{... | collective-permute-start | bytes 49160 | tf_op jit(solution)/shard_map/ppermute | solution.py:106
  60.5 26.5 %collective-permute-start = (bf16[12,1,128,128]{3,2,1,0:T(8,128)(2,1)}, bf16[12,1,128,128]{3,2,1,0:T(8,128)(2,1)}, u32[]{:S(2)}, u32[]{:S(2)}) collective-permute-start(bf16[12,1,128,128]{3,2,1,0:T(8,128)(2,1)} %slice.7), channel_id=1, source_target_pairs={{0,4},{4,0},{8,12},{12,8},{16,20},{20,16},{24,28},{28,24},{1,5},{5... | collective-permute-start | bytes 1179656 | tf_op jit(solution)/shard_map/ppermute | solution.py:15
  62.7 7.0 %collective-permute-start.3 = (bf16[16,512]{1,0:T(8,128)(2,1)S(1)}, bf16[16,512]{1,0:T(8,128)(2,1)S(1)}, u32[]{:S(2)}, u32[]{:S(2)}) collective-permute-start(bf16[16,512]{1,0:T(8,128)(2,1)S(1)} %collective-permute-done.1), channel_id=1, source_target_pairs={{0,4},{4,8},{8,12},{12,16},{16,20},{20,24},{24,28},{28,0},{1,5},{5... | collective-permute-start | bytes 49160 | tf_op jit(solution)/shard_map/ppermute | solution.py:103
  64.8 7.4 %collective-permute-start.4 = (bf16[16,512]{1,0:T(8,128)(2,1)S(1)}, bf16[16,512]{1,0:T(8,128)(2,1)S(1)}, u32[]{:S(2)}, u32[]{:S(2)}) collective-permute-start(bf16[16,512]{1,0:T(8,128)(2,1)S(1)} %collective-permute-done.2), channel_id=1, source_target_pairs={{0,28},{4,0},{8,4},{12,8},{16,12},{20,16},{24,20},{28,24},{1,29},{... | collective-permute-start | bytes 49160 | tf_op jit(solution)/shard_map/ppermute | solution.py:106
  69.7 6.4 %collective-permute-start.5 = (bf16[16,512]{1,0:T(8,128)(2,1)S(1)}, bf16[16,512]{1,0:T(8,128)(2,1)S(1)}, u32[]{:S(2)}, u32[]{:S(2)}) collective-permute-start(bf16[16,512]{1,0:T(8,128)(2,1)S(1)} %collective-permute-done.3), channel_id=1, source_target_pairs={{0,4},{4,8},{8,12},{12,16},{16,20},{20,24},{24,28},{28,0},{1,5},{5... | collective-permute-start | bytes 49160 | tf_op jit(solution)/shard_map/ppermute | solution.py:103
  72.2 4.0 %collective-permute-start.6 = (bf16[16,512]{1,0:T(8,128)(2,1)S(1)}, bf16[16,512]{1,0:T(8,128)(2,1)S(1)}, u32[]{:S(2)}, u32[]{:S(2)}) collective-permute-start(bf16[16,512]{1,0:T(8,128)(2,1)S(1)} %collective-permute-done.4), channel_id=1, source_target_pairs={{0,28},{4,0},{8,4},{12,8},{16,12},{20,16},{24,20},{28,24},{1,29},{... | collective-permute-start | bytes 49160 | tf_op jit(solution)/shard_map/ppermute | solution.py:106
  76.2 6.4 %collective-permute-start.7 = (bf16[16,512]{1,0:T(8,128)(2,1)S(1)}, bf16[16,512]{1,0:T(8,128)(2,1)S(1)}, u32[]{:S(2)}, u32[]{:S(2)}) collective-permute-start(bf16[16,512]{1,0:T(8,128)(2,1)S(1)} %collective-permute-done.5), channel_id=1, source_target_pairs={{0,4},{4,8},{8,12},{12,16},{16,20},{20,24},{24,28},{28,0},{1,5},{5... | collective-permute-start | bytes 49160 | tf_op jit(solution)/shard_map/ppermute | solution.py:103
  113.9 7.0 %copy-start = (f32[12,128,128]{2,1,0:T(8,128)S(1)}, f32[12,128,128]{2,1,0:T(8,128)}, u32[]{:S(2)}) copy-start(f32[12,128,128]{2,1,0:T(8,128)} %copy.128) | copy-start | bytes 2359300
  166.5 5.0 %collective-permute-start.8 = (bf16[12,32,128]{2,0,1:T(8,128)(2,1)S(1)}, bf16[12,32,128]{2,0,1:T(8,128)(2,1)S(1)}, u32[]{:S(2)}, u32[]{:S(2)}) collective-permute-start(bf16[12,32,128]{2,0,1:T(8,128)(2,1)S(1)} %copy.144), channel_id=1, source_target_pairs={{0,4},{4,0},{8,12},{12,8},{16,20},{20,16},{24,28},{28,24},{1,5},{5... | collective-permute-start | bytes 294920 | tf_op jit(solution)/shard_map/ppermute | solution.py:15
